TPU v7x, 128 devices: a whole 4x4x4 slice. The times are simulated.
128 devices in a mesh: ctx: 8 (over y_lo, z), fsdp: 16 (over y_hi, x, core).
Axes of the slice: x: 4, y: 4 (y_hi: 2, y_lo: 2; y = y_hi * 2 + y_lo), z: 4, core: 2. Of those that a mesh axis runs over, the one named last changes fastest.
Arguments:
- hidden: bfloat16 [16384, 16384], P('ctx', 'fsdp'), may hold values from -48 to 48
- w_query: bfloat16 [16384, 2048], P('fsdp'), may hold values from -0.0625 to 0.0625
- w_key_value: bfloat16 [16384, 256], P('fsdp'), may hold values from -0.046875 to 0.046875
- block_doc: int32 [32], replicated, may hold values from 0 to 7, never falling along the last dimension, each value on 1 to 16 neighbouring positions
Outputs:
- attended: bfloat16 [16384, 2048], P('ctx', 'fsdp')
Inputs may be any that keep to these rules, and one draw needn't show every extreme that they name: `block_doc`: document ids never fall along the context; each document covers 1 to 16 blocks, one exactly 16.
All inputs are finite; a program needn't handle non-finite values.
Results may differ from a plain program's by a relative error of at most 0.01.
The roundings to bfloat16 on the way count: a program that leaves them out, or rounds other values in their place, can miss the bound.
Values may be sent and summed in bfloat16 or wider, within the bound.
No kernel may reach another device: no remote copies, remote signals or barrier semaphores. Data moves between devices by JAX's collectives and lax.ppermute only.
A program may use at most 384 MiB of HBM per device.

v0:
```python
import jax
import jax.numpy as jnp
from jax import lax
from jax.sharding import PartitionSpec as P

DH = 128
HQ = 16
BLOCK = 512


masked_low = -1e30


def shifted(array, axis, by):
    count = lax.axis_size(axis)
    return lax.ppermute(array, axis, [(i, (i + by) % count) for i in range(count)])


def rotate_pairs(vectors, positions):
    half_dim = DH // 2
    frequency = 500000.0 ** (-2.0 * jnp.arange(half_dim, dtype=jnp.float32) / DH)
    angles = positions[:, None].astype(jnp.float32) * frequency[None, :]
    cosine = jnp.cos(angles)
    sine = jnp.sin(angles)
    first_half = vectors[..., :half_dim]
    second_half = vectors[..., half_dim:]
    return jnp.concatenate(
        [first_half * cosine - second_half * sine, second_half * cosine + first_half * sine], -1
    )


def document_of(positions, block_doc):
    block_ids = positions // BLOCK
    table_ids = jnp.arange(block_doc.shape[0], dtype=jnp.int32)
    matches = block_ids[:, None] == table_ids[None, :]
    return jnp.sum(jnp.where(matches, block_doc[None, :], 0), axis=1)


def attend_tile(state_in, query_rows, query_pos, key_rows, value_rows, key_pos, block_doc):
    allowed = (key_pos[None, :] <= query_pos[:, None]) & (
        document_of(query_pos, block_doc)[:, None] == document_of(key_pos, block_doc)[None, :]
    )
    scale = DH ** (-0.5)
    run_max, run_sum, run_out = state_in
    scores = (
        jnp.einsum("hqe,ke->hqk", query_rows, key_rows, preferred_element_type=jnp.float32) * scale
    )
    scores = jnp.where(allowed[None], scores, masked_low)
    new_max = jnp.maximum(run_max, jnp.max(scores, axis=-1))
    weights_f = jnp.where(allowed[None], jnp.exp(scores - new_max[..., None]), 0.0)
    rescale = jnp.exp(run_max - new_max)
    new_sum = run_sum * rescale + jnp.sum(weights_f, axis=-1)
    new_out = run_out * rescale[..., None] + jnp.einsum(
        "hqk,ke->hqe",
        weights_f.astype(jnp.bfloat16),
        value_rows,
        preferred_element_type=jnp.float32,
    )
    return (new_max, new_sum, new_out)


def on_device(hidden, w_query, w_key_value, block_doc):
    tok_rows = hidden.shape[0]
    heads_dev = HQ // lax.axis_size("fsdp")
    columns = w_query
    columns = columns.reshape(columns.shape[0], heads_dev * lax.axis_size("fsdp"), DH)
    query = lax.psum_scatter(
        jnp.einsum("td,dhe->hte", hidden, columns, preferred_element_type=jnp.float32),
        "fsdp",
        scatter_dimension=0,
        tiled=True,
    )
    key_vals = lax.psum(jnp.dot(hidden, w_key_value, preferred_element_type=jnp.float32), "fsdp")
    own_index = lax.axis_index("ctx")
    local_range = jnp.arange(tok_rows, dtype=jnp.int32)
    positions = own_index * tok_rows + local_range
    q_rot = rotate_pairs(query, positions).astype(jnp.bfloat16)
    keys = rotate_pairs(key_vals[:, :DH], positions).astype(jnp.bfloat16)
    values = key_vals[:, DH:].astype(jnp.bfloat16)
    start_state = (
        jnp.full((heads_dev, tok_rows), masked_low, jnp.float32),
        jnp.zeros((heads_dev, tok_rows), jnp.float32),
        jnp.zeros((heads_dev, tok_rows, DH), jnp.float32),
    )
    ctx_count = lax.axis_size("ctx")

    def cycle_step(step_index, carried):
        query_rows, run_max, run_sum, run_out = carried
        owner = (own_index - step_index) % ctx_count
        query_pos = owner * tok_rows + local_range
        run_max, run_sum, run_out = attend_tile(
            (run_max, run_sum, run_out), query_rows, query_pos, keys, values, positions, block_doc
        )
        query_rows = shifted(query_rows, "ctx", 1)
        run_max, run_sum, run_out = shifted((run_max, run_sum, run_out), "ctx", 1)
        return (query_rows, run_max, run_sum, run_out)

    final_state = lax.fori_loop(0, ctx_count, cycle_step, (q_rot,) + start_state)
    run_max, run_sum, run_out = (final_state[1], final_state[2], final_state[3])
    attended = (run_out / run_sum[..., None]).astype(jnp.bfloat16)
    return jnp.transpose(attended, (1, 0, 2)).reshape(tok_rows, heads_dev * DH)


def solution(mesh):
    return jax.shard_map(
        on_device,
        mesh=mesh,
        in_specs=(P("ctx", "fsdp"), P("fsdp", None), P("fsdp", None), P()),
        out_specs=P("ctx", "fsdp"),
        check_vma=False,
    )
```

profile of v0, /device:TPU:40, one launch (start us, length us, event | category | flops | bytes accessed | tf_op | source)
XLA Modules:
  0.0 750.5 jit_solution(6649314416705663610)
XLA Ops:
  6.5 1.0 copy-done
  7.6 4.8 fusion.52
  12.5 6.4 copy.17
  18.9 15.3 %convolution_bitcast_fusion = f32[16,2048,128]{1,2,0:T(8,128)} fusion(bf16[1024,16,128]{0,2,1:T(8,128)(2,1)} %bitcast.46, bf16[2048,1024]{1,0:T(8,128)(2,1)} %param.6), kind=kOutput, calls=%fused_computation.46 | convolution fusion | flops 8589934592 | bytes 25165824 | tf_op jit(solution)/shard_map/td,dhe->hte/dot_general | solution.py:68
  34.2 124.1 %all-reduce.2.cloned.1.call-done = f32[2048,256]{0,1:T(8,128)} async-done(((f32[2048,256]{0,1:T(8,128)}), f32[2048,256]{0,1:T(8,128)}) %all-reduce.2.cloned.1.call-update) | async-done | bytes 2097168 | tf_op jit(solution)/shard_map/psum | solution.py:73
  158.4 3.7 fusion.44
  162.4 1.3 slice.38
  163.7 1.0 copy.15
  164.7 145.9 %reduce-scatter.2.cloned.1.call-done = f32[1,2048,128]{1,2,0:T(8,128)} async-done(((f32[16,2048,128]{1,2,0:T(8,128)}), f32[1,2048,128]{1,2,0:T(8,128)}) %reduce-scatter.2.cloned.1.call-update) | async-done | bytes 1048592 | tf_op jit(solution)/shard_map/reduce_scatter | solution.py:67
  310.6 3.7 fusion.48
  314.7 427.8 %while.24 = (s32[]{:T(128)}, bf16[1,2048,128]{2,1,0:T(8,128)(2,1)S(1)}, f32[1,2048]{1,0:T(1,128)S(1)}, f32[1,2048]{1,0:T(1,128)S(1)}, f32[1,2048,128]{2,1,0:T(8,...) while((s32[]{:T(128)}, ...), condition=%wide.region_7.8_spmd.clone.clone, body=%wide.region_2.7_spmd.clone.clone.sunk | while | flops 2240745472 | bytes 63803996 | solution.py:98
  315.3 4.0 fusion.69
  319.3 7.5 fusion.70
  326.8 6.9 fusion.71
  333.7 1.6 collective-permute-start.3
  335.3 1.3 collective-permute-start
  336.5 1.1 collective-permute-start.1
  337.7 1.6 collective-permute-start.2
  339.2 30.3 %collective-permute-done.1 = f32[1,2048]{1,0:T(1,128)S(1)} collective-permute-done((f32[1,2048]{1,0:T(1,128)S(1)}, f32[1,2048]{1,0:T(1,128)S(1)}, u32[]{:S(2)}, u32[]{:S(2)}) %collective-permute-start.1) | collective-permute-done | bytes 8224 | tf_op jit(solution)/shard_map/while/body/eval_jaxpr/ppermute | solution.py:16
  370.0 4.0 fusion.69
  374.1 7.5 fusion.70
  381.6 6.9 fusion.71
  388.5 1.6 collective-permute-start.3
  390.0 1.3 collective-permute-start
  391.3 3.3 collective-permute-start.1
  394.6 29.7 %collective-permute-done.1 = f32[1,2048]{1,0:T(1,128)S(1)} collective-permute-done((f32[1,2048]{1,0:T(1,128)S(1)}, f32[1,2048]{1,0:T(1,128)S(1)}, u32[]{:S(2)}, u32[]{:S(2)}) %collective-permute-start.1) | collective-permute-done | bytes 8224 | tf_op jit(solution)/shard_map/while/body/eval_jaxpr/ppermute | solution.py:16
  424.7 4.0 fusion.69
  428.8 7.5 fusion.70
  436.3 6.9 fusion.71
  443.2 0.7 collective-permute-start.3
  443.9 2.0 collective-permute-start
  446.0 4.6 collective-permute-start.1
  450.6 28.8 %collective-permute-done.1 = f32[1,2048]{1,0:T(1,128)S(1)} collective-permute-done((f32[1,2048]{1,0:T(1,128)S(1)}, f32[1,2048]{1,0:T(1,128)S(1)}, u32[]{:S(2)}, u32[]{:S(2)}) %collective-permute-start.1) | collective-permute-done | bytes 8224 | tf_op jit(solution)/shard_map/while/body/eval_jaxpr/ppermute | solution.py:16
  479.9 4.0 fusion.69
  483.9 7.5 fusion.70
  491.4 6.9 fusion.71
  498.4 2.8 collective-permute-start
  501.2 4.6 collective-permute-start.1
  505.8 28.0 %collective-permute-done.1 = f32[1,2048]{1,0:T(1,128)S(1)} collective-permute-done((f32[1,2048]{1,0:T(1,128)S(1)}, f32[1,2048]{1,0:T(1,128)S(1)}, u32[]{:S(2)}, u32[]{:S(2)}) %collective-permute-start.1) | collective-permute-done | bytes 8224 | tf_op jit(solution)/shard_map/while/body/eval_jaxpr/ppermute | solution.py:16
  534.2 4.0 fusion.69
  538.2 7.5 fusion.70
  545.7 6.9 fusion.71
  552.7 2.8 collective-permute-start
  555.5 4.6 collective-permute-start.1
  560.1 27.1 %collective-permute-done.1 = f32[1,2048]{1,0:T(1,128)S(1)} collective-permute-done((f32[1,2048]{1,0:T(1,128)S(1)}, f32[1,2048]{1,0:T(1,128)S(1)}, u32[]{:S(2)}, u32[]{:S(2)}) %collective-permute-start.1) | collective-permute-done | bytes 8224 | tf_op jit(solution)/shard_map/while/body/eval_jaxpr/ppermute | solution.py:16
  587.6 4.0 fusion.69
  591.7 7.5 fusion.70
  599.2 6.9 fusion.71
  606.1 2.8 collective-permute-start
  608.9 4.6 collective-permute-start.1
  613.5 26.2 %collective-permute-done.1 = f32[1,2048]{1,0:T(1,128)S(1)} collective-permute-done((f32[1,2048]{1,0:T(1,128)S(1)}, f32[1,2048]{1,0:T(1,128)S(1)}, u32[]{:S(2)}, u32[]{:S(2)}) %collective-permute-start.1) | collective-permute-done | bytes 8224 | tf_op jit(solution)/shard_map/while/body/eval_jaxpr/ppermute | solution.py:16
  640.2 4.0 fusion.69
  644.3 7.5 fusion.70
  651.8 6.9 fusion.71
  658.7 2.9 collective-permute-start
  661.6 4.6 collective-permute-start.1
  666.2 25.4 %collective-permute-done.1 = f32[1,2048]{1,0:T(1,128)S(1)} collective-permute-done((f32[1,2048]{1,0:T(1,128)S(1)}, f32[1,2048]{1,0:T(1,128)S(1)}, u32[]{:S(2)}, u32[]{:S(2)}) %collective-permute-start.1) | collective-permute-done | bytes 8224 | tf_op jit(solution)/shard_map/while/body/eval_jaxpr/ppermute | solution.py:16
  692.0 4.0 fusion.69
  696.0 7.5 fusion.70
  703.5 6.9 fusion.71
  710.4 2.9 collective-permute-start
  713.3 4.6 collective-permute-start.1
  717.9 24.5 %collective-permute-done.1 = f32[1,2048]{1,0:T(1,128)S(1)} collective-permute-done((f32[1,2048]{1,0:T(1,128)S(1)}, f32[1,2048]{1,0:T(1,128)S(1)}, u32[]{:S(2)}, u32[]{:S(2)}) %collective-permute-start.1) | collective-permute-done | bytes 8224 | tf_op jit(solution)/shard_map/while/body/eval_jaxpr/ppermute | solution.py:16
  742.5 1.1 fusion.51
  (132 shorter events, 4.3 us)
Async XLA Ops:
  6.5 1.0 copy-start
  6.5 151.8 %all-reduce.2.cloned.1.call-start = ((), (), s32[]{:S(2)}) async-start(), calls=%async_computation.2 | async-start | bytes 4194304 | tf_op jit(solution)/shard_map/psum | solution.py:73
  12.4 298.2 %reduce-scatter.2.cloned.1.call-start = ((), (), s32[]{:S(2)}) async-start(), calls=%async_computation.1 | async-start | bytes 17825792 | tf_op jit(solution)/shard_map/reduce_scatter | solution.py:67
  34.2 280.5 %copy-start.2 = (s32[32]{0:T(128)S(1)}, s32[32]{0:T(128)}, u32[]{:S(2)}) copy-start(s32[32]{0:T(128)} %param.9) | copy-start | bytes 388
  315.2 11.6 %copy-start.1 = (bf16[2048,128]{1,0:T(8,128)(2,1)S(1)}, bf16[2048,128]{1,0:T(8,128)(2,1)}, u32[]{:S(2)}) copy-start(bf16[2048,128]{1,0:T(8,128)(2,1)} %get-tuple-element.578) | copy-start | bytes 1572868 | tf_op jit(solution)/shard_map/while
  333.7 35.9 %collective-permute-start.3 = (f32[1,2048,128]{2,1,0:T(8,128)}, f32[1,2048,128]{2,1,0:T(8,128)S(1)}, u32[]{:S(2)}, u32[]{:S(2)}) collective-permute-start(f32[1,2048,128]{2,1,0:T(8,128)} %fusion.71), channel_id=1, source_target_pairs={{0,16},{16,32},{32,48},{48,64},{64,80},{80,96},{96,112},{112,0},{1... | collective-permute-start | bytes 3145736 | tf_op jit(solution)/shard_map/while/body/eval_jaxpr/ppermute | solution.py:16
  335.3 34.4 %collective-permute-start = (bf16[1,2048,128]{2,1,0:T(8,128)(2,1)S(1)}, bf16[1,2048,128]{2,1,0:T(8,128)(2,1)S(1)}, u32[]{:S(2)}, u32[]{:S(2)}) collective-permute-start(bf16[1,2048,128]{2,1,0:T(8,128)(2,1)S(1)} %copy.25), channel_id=1, source_target_pairs={{0,16},{16,32},{32,48},{48,64},{64,80},{80,96},{96,112},{112,0},{1... | collective-permute-start | bytes 1572872 | tf_op jit(solution)/shard_map/while/body/eval_jaxpr/ppermute | solution.py:16
  336.5 33.0 %collective-permute-start.1 = (f32[1,2048]{1,0:T(1,128)S(1)}, f32[1,2048]{1,0:T(1,128)S(1)}, u32[]{:S(2)}, u32[]{:S(2)}) collective-permute-start(f32[1,2048]{1,0:T(1,128)S(1)} %max.14), channel_id=1, source_target_pairs={{0,16},{16,32},{32,48},{48,64},{64,80},{80,96},{96,112},{112,0},{1... | collective-permute-start | bytes 24584 | tf_op jit(solution)/shard_map/while/body/eval_jaxpr/ppermute | solution.py:16
  337.7 32.0 %collective-permute-start.2 = (f32[1,2048]{1,0:T(1,128)S(1)}, f32[1,2048]{1,0:T(1,128)S(1)}, u32[]{:S(2)}, u32[]{:S(2)}) collective-permute-start(f32[1,2048]{1,0:T(1,128)S(1)} %get-tuple-element.538), channel_id=1, source_target_pairs={{0,16},{16,32},{32,48},{48,64},{64,80},{80,96},{96,112},{112,0},{1... | collective-permute-start | bytes 24584 | tf_op jit(solution)/shard_map/while/body/eval_jaxpr/ppermute | solution.py:16
  370.0 11.6 %copy-start.1 = (bf16[2048,128]{1,0:T(8,128)(2,1)S(1)}, bf16[2048,128]{1,0:T(8,128)(2,1)}, u32[]{:S(2)}) copy-start(bf16[2048,128]{1,0:T(8,128)(2,1)} %get-tuple-element.578) | copy-start | bytes 1572868 | tf_op jit(solution)/shard_map/while
  388.5 35.9 %collective-permute-start.3 = (f32[1,2048,128]{2,1,0:T(8,128)}, f32[1,2048,128]{2,1,0:T(8,128)S(1)}, u32[]{:S(2)}, u32[]{:S(2)}) collective-permute-start(f32[1,2048,128]{2,1,0:T(8,128)} %fusion.71), channel_id=1, source_target_pairs={{0,16},{16,32},{32,48},{48,64},{64,80},{80,96},{96,112},{112,0},{1... | collective-permute-start | bytes 3145736 | tf_op jit(solution)/shard_map/while/body/eval_jaxpr/ppermute | solution.py:16
  390.0 34.4 %collective-permute-start = (bf16[1,2048,128]{2,1,0:T(8,128)(2,1)S(1)}, bf16[1,2048,128]{2,1,0:T(8,128)(2,1)S(1)}, u32[]{:S(2)}, u32[]{:S(2)}) collective-permute-start(bf16[1,2048,128]{2,1,0:T(8,128)(2,1)S(1)} %copy.25), channel_id=1, source_target_pairs={{0,16},{16,32},{32,48},{48,64},{64,80},{80,96},{96,112},{112,0},{1... | collective-permute-start | bytes 1572872 | tf_op jit(solution)/shard_map/while/body/eval_jaxpr/ppermute | solution.py:16
  391.3 33.0 %collective-permute-start.1 = (f32[1,2048]{1,0:T(1,128)S(1)}, f32[1,2048]{1,0:T(1,128)S(1)}, u32[]{:S(2)}, u32[]{:S(2)}) collective-permute-start(f32[1,2048]{1,0:T(1,128)S(1)} %max.14), channel_id=1, source_target_pairs={{0,16},{16,32},{32,48},{48,64},{64,80},{80,96},{96,112},{112,0},{1... | collective-permute-start | bytes 24584 | tf_op jit(solution)/shard_map/while/body/eval_jaxpr/ppermute | solution.py:16
  394.6 29.8 %collective-permute-start.2 = (f32[1,2048]{1,0:T(1,128)S(1)}, f32[1,2048]{1,0:T(1,128)S(1)}, u32[]{:S(2)}, u32[]{:S(2)}) collective-permute-start(f32[1,2048]{1,0:T(1,128)S(1)} %get-tuple-element.538), channel_id=1, source_target_pairs={{0,16},{16,32},{32,48},{48,64},{64,80},{80,96},{96,112},{112,0},{1... | collective-permute-start | bytes 24584 | tf_op jit(solution)/shard_map/while/body/eval_jaxpr/ppermute | solution.py:16
  424.7 11.6 %copy-start.1 = (bf16[2048,128]{1,0:T(8,128)(2,1)S(1)}, bf16[2048,128]{1,0:T(8,128)(2,1)}, u32[]{:S(2)}) copy-start(bf16[2048,128]{1,0:T(8,128)(2,1)} %get-tuple-element.578) | copy-start | bytes 1572868 | tf_op jit(solution)/shard_map/while
  443.2 36.3 %collective-permute-start.3 = (f32[1,2048,128]{2,1,0:T(8,128)}, f32[1,2048,128]{2,1,0:T(8,128)S(1)}, u32[]{:S(2)}, u32[]{:S(2)}) collective-permute-start(f32[1,2048,128]{2,1,0:T(8,128)} %fusion.71), channel_id=1, source_target_pairs={{0,16},{16,32},{32,48},{48,64},{64,80},{80,96},{96,112},{112,0},{1... | collective-permute-start | bytes 3145736 | tf_op jit(solution)/shard_map/while/body/eval_jaxpr/ppermute | solution.py:16
  443.9 35.6 %collective-permute-start = (bf16[1,2048,128]{2,1,0:T(8,128)(2,1)S(1)}, bf16[1,2048,128]{2,1,0:T(8,128)(2,1)S(1)}, u32[]{:S(2)}, u32[]{:S(2)}) collective-permute-start(bf16[1,2048,128]{2,1,0:T(8,128)(2,1)S(1)} %copy.25), channel_id=1, source_target_pairs={{0,16},{16,32},{32,48},{48,64},{64,80},{80,96},{96,112},{112,0},{1... | collective-permute-start | bytes 1572872 | tf_op jit(solution)/shard_map/while/body/eval_jaxpr/ppermute | solution.py:16
  446.0 33.5 %collective-permute-start.1 = (f32[1,2048]{1,0:T(1,128)S(1)}, f32[1,2048]{1,0:T(1,128)S(1)}, u32[]{:S(2)}, u32[]{:S(2)}) collective-permute-start(f32[1,2048]{1,0:T(1,128)S(1)} %max.14), channel_id=1, source_target_pairs={{0,16},{16,32},{32,48},{48,64},{64,80},{80,96},{96,112},{112,0},{1... | collective-permute-start | bytes 24584 | tf_op jit(solution)/shard_map/while/body/eval_jaxpr/ppermute | solution.py:16
  450.6 29.0 %collective-permute-start.2 = (f32[1,2048]{1,0:T(1,128)S(1)}, f32[1,2048]{1,0:T(1,128)S(1)}, u32[]{:S(2)}, u32[]{:S(2)}) collective-permute-start(f32[1,2048]{1,0:T(1,128)S(1)} %get-tuple-element.538), channel_id=1, source_target_pairs={{0,16},{16,32},{32,48},{48,64},{64,80},{80,96},{96,112},{112,0},{1... | collective-permute-start | bytes 24584 | tf_op jit(solution)/shard_map/while/body/eval_jaxpr/ppermute | solution.py:16
  479.9 11.6 %copy-start.1 = (bf16[2048,128]{1,0:T(8,128)(2,1)S(1)}, bf16[2048,128]{1,0:T(8,128)(2,1)}, u32[]{:S(2)}) copy-start(bf16[2048,128]{1,0:T(8,128)(2,1)} %get-tuple-element.578) | copy-start | bytes 1572868 | tf_op jit(solution)/shard_map/while
  498.4 35.5 %collective-permute-start.3 = (f32[1,2048,128]{2,1,0:T(8,128)}, f32[1,2048,128]{2,1,0:T(8,128)S(1)}, u32[]{:S(2)}, u32[]{:S(2)}) collective-permute-start(f32[1,2048,128]{2,1,0:T(8,128)} %fusion.71), channel_id=1, source_target_pairs={{0,16},{16,32},{32,48},{48,64},{64,80},{80,96},{96,112},{112,0},{1... | collective-permute-start | bytes 3145736 | tf_op jit(solution)/shard_map/while/body/eval_jaxpr/ppermute | solution.py:16
  498.4 35.5 %collective-permute-start = (bf16[1,2048,128]{2,1,0:T(8,128)(2,1)S(1)}, bf16[1,2048,128]{2,1,0:T(8,128)(2,1)S(1)}, u32[]{:S(2)}, u32[]{:S(2)}) collective-permute-start(bf16[1,2048,128]{2,1,0:T(8,128)(2,1)S(1)} %copy.25), channel_id=1, source_target_pairs={{0,16},{16,32},{32,48},{48,64},{64,80},{80,96},{96,112},{112,0},{1... | collective-permute-start | bytes 1572872 | tf_op jit(solution)/shard_map/while/body/eval_jaxpr/ppermute | solution.py:16
  501.2 32.6 %collective-permute-start.1 = (f32[1,2048]{1,0:T(1,128)S(1)}, f32[1,2048]{1,0:T(1,128)S(1)}, u32[]{:S(2)}, u32[]{:S(2)}) collective-permute-start(f32[1,2048]{1,0:T(1,128)S(1)} %max.14), channel_id=1, source_target_pairs={{0,16},{16,32},{32,48},{48,64},{64,80},{80,96},{96,112},{112,0},{1... | collective-permute-start | bytes 24584 | tf_op jit(solution)/shard_map/while/body/eval_jaxpr/ppermute | solution.py:16
  505.7 28.1 %collective-permute-start.2 = (f32[1,2048]{1,0:T(1,128)S(1)}, f32[1,2048]{1,0:T(1,128)S(1)}, u32[]{:S(2)}, u32[]{:S(2)}) collective-permute-start(f32[1,2048]{1,0:T(1,128)S(1)} %get-tuple-element.538), channel_id=1, source_target_pairs={{0,16},{16,32},{32,48},{48,64},{64,80},{80,96},{96,112},{112,0},{1... | collective-permute-start | bytes 24584 | tf_op jit(solution)/shard_map/while/body/eval_jaxpr/ppermute | solution.py:16
  534.2 11.6 %copy-start.1 = (bf16[2048,128]{1,0:T(8,128)(2,1)S(1)}, bf16[2048,128]{1,0:T(8,128)(2,1)}, u32[]{:S(2)}) copy-start(bf16[2048,128]{1,0:T(8,128)(2,1)} %get-tuple-element.578) | copy-start | bytes 1572868 | tf_op jit(solution)/shard_map/while
  552.7 34.6 %collective-permute-start.3 = (f32[1,2048,128]{2,1,0:T(8,128)}, f32[1,2048,128]{2,1,0:T(8,128)S(1)}, u32[]{:S(2)}, u32[]{:S(2)}) collective-permute-start(f32[1,2048,128]{2,1,0:T(8,128)} %fusion.71), channel_id=1, source_target_pairs={{0,16},{16,32},{32,48},{48,64},{64,80},{80,96},{96,112},{112,0},{1... | collective-permute-start | bytes 3145736 | tf_op jit(solution)/shard_map/while/body/eval_jaxpr/ppermute | solution.py:16
  552.7 34.6 %collective-permute-start = (bf16[1,2048,128]{2,1,0:T(8,128)(2,1)S(1)}, bf16[1,2048,128]{2,1,0:T(8,128)(2,1)S(1)}, u32[]{:S(2)}, u32[]{:S(2)}) collective-permute-start(bf16[1,2048,128]{2,1,0:T(8,128)(2,1)S(1)} %copy.25), channel_id=1, source_target_pairs={{0,16},{16,32},{32,48},{48,64},{64,80},{80,96},{96,112},{112,0},{1... | collective-permute-start | bytes 1572872 | tf_op jit(solution)/shard_map/while/body/eval_jaxpr/ppermute | solution.py:16
  555.5 31.7 %collective-permute-start.1 = (f32[1,2048]{1,0:T(1,128)S(1)}, f32[1,2048]{1,0:T(1,128)S(1)}, u32[]{:S(2)}, u32[]{:S(2)}) collective-permute-start(f32[1,2048]{1,0:T(1,128)S(1)} %max.14), channel_id=1, source_target_pairs={{0,16},{16,32},{32,48},{48,64},{64,80},{80,96},{96,112},{112,0},{1... | collective-permute-start | bytes 24584 | tf_op jit(solution)/shard_map/while/body/eval_jaxpr/ppermute | solution.py:16
  560.1 27.2 %collective-permute-start.2 = (f32[1,2048]{1,0:T(1,128)S(1)}, f32[1,2048]{1,0:T(1,128)S(1)}, u32[]{:S(2)}, u32[]{:S(2)}) collective-permute-start(f32[1,2048]{1,0:T(1,128)S(1)} %get-tuple-element.538), channel_id=1, source_target_pairs={{0,16},{16,32},{32,48},{48,64},{64,80},{80,96},{96,112},{112,0},{1... | collective-permute-start | bytes 24584 | tf_op jit(solution)/shard_map/while/body/eval_jaxpr/ppermute | solution.py:16
  587.6 11.6 %copy-start.1 = (bf16[2048,128]{1,0:T(8,128)(2,1)S(1)}, bf16[2048,128]{1,0:T(8,128)(2,1)}, u32[]{:S(2)}) copy-start(bf16[2048,128]{1,0:T(8,128)(2,1)} %get-tuple-element.578) | copy-start | bytes 1572868 | tf_op jit(solution)/shard_map/while
  606.1 33.8 %collective-permute-start.3 = (f32[1,2048,128]{2,1,0:T(8,128)}, f32[1,2048,128]{2,1,0:T(8,128)S(1)}, u32[]{:S(2)}, u32[]{:S(2)}) collective-permute-start(f32[1,2048,128]{2,1,0:T(8,128)} %fusion.71), channel_id=1, source_target_pairs={{0,16},{16,32},{32,48},{48,64},{64,80},{80,96},{96,112},{112,0},{1... | collective-permute-start | bytes 3145736 | tf_op jit(solution)/shard_map/while/body/eval_jaxpr/ppermute | solution.py:16
  606.1 33.8 %collective-permute-start = (bf16[1,2048,128]{2,1,0:T(8,128)(2,1)S(1)}, bf16[1,2048,128]{2,1,0:T(8,128)(2,1)S(1)}, u32[]{:S(2)}, u32[]{:S(2)}) collective-permute-start(bf16[1,2048,128]{2,1,0:T(8,128)(2,1)S(1)} %copy.25), channel_id=1, source_target_pairs={{0,16},{16,32},{32,48},{48,64},{64,80},{80,96},{96,112},{112,0},{1... | collective-permute-start | bytes 1572872 | tf_op jit(solution)/shard_map/while/body/eval_jaxpr/ppermute | solution.py:16
  608.9 30.8 %collective-permute-start.1 = (f32[1,2048]{1,0:T(1,128)S(1)}, f32[1,2048]{1,0:T(1,128)S(1)}, u32[]{:S(2)}, u32[]{:S(2)}) collective-permute-start(f32[1,2048]{1,0:T(1,128)S(1)} %max.14), channel_id=1, source_target_pairs={{0,16},{16,32},{32,48},{48,64},{64,80},{80,96},{96,112},{112,0},{1... | collective-permute-start | bytes 24584 | tf_op jit(solution)/shard_map/while/body/eval_jaxpr/ppermute | solution.py:16
  613.5 26.3 %collective-permute-start.2 = (f32[1,2048]{1,0:T(1,128)S(1)}, f32[1,2048]{1,0:T(1,128)S(1)}, u32[]{:S(2)}, u32[]{:S(2)}) collective-permute-start(f32[1,2048]{1,0:T(1,128)S(1)} %get-tuple-element.538), channel_id=1, source_target_pairs={{0,16},{16,32},{32,48},{48,64},{64,80},{80,96},{96,112},{112,0},{1... | collective-permute-start | bytes 24584 | tf_op jit(solution)/shard_map/while/body/eval_jaxpr/ppermute | solution.py:16
  640.2 11.6 %copy-start.1 = (bf16[2048,128]{1,0:T(8,128)(2,1)S(1)}, bf16[2048,128]{1,0:T(8,128)(2,1)}, u32[]{:S(2)}) copy-start(bf16[2048,128]{1,0:T(8,128)(2,1)} %get-tuple-element.578) | copy-start | bytes 1572868 | tf_op jit(solution)/shard_map/while
  658.7 32.9 %collective-permute-start.3 = (f32[1,2048,128]{2,1,0:T(8,128)}, f32[1,2048,128]{2,1,0:T(8,128)S(1)}, u32[]{:S(2)}, u32[]{:S(2)}) collective-permute-start(f32[1,2048,128]{2,1,0:T(8,128)} %fusion.71), channel_id=1, source_target_pairs={{0,16},{16,32},{32,48},{48,64},{64,80},{80,96},{96,112},{112,0},{1... | collective-permute-start | bytes 3145736 | tf_op jit(solution)/shard_map/while/body/eval_jaxpr/ppermute | solution.py:16
  658.7 32.9 %collective-permute-start = (bf16[1,2048,128]{2,1,0:T(8,128)(2,1)S(1)}, bf16[1,2048,128]{2,1,0:T(8,128)(2,1)S(1)}, u32[]{:S(2)}, u32[]{:S(2)}) collective-permute-start(bf16[1,2048,128]{2,1,0:T(8,128)(2,1)S(1)} %copy.25), channel_id=1, source_target_pairs={{0,16},{16,32},{32,48},{48,64},{64,80},{80,96},{96,112},{112,0},{1... | collective-permute-start | bytes 1572872 | tf_op jit(solution)/shard_map/while/body/eval_jaxpr/ppermute | solution.py:16
  661.6 30.0 %collective-permute-start.1 = (f32[1,2048]{1,0:T(1,128)S(1)}, f32[1,2048]{1,0:T(1,128)S(1)}, u32[]{:S(2)}, u32[]{:S(2)}) collective-permute-start(f32[1,2048]{1,0:T(1,128)S(1)} %max.14), channel_id=1, source_target_pairs={{0,16},{16,32},{32,48},{48,64},{64,80},{80,96},{96,112},{112,0},{1... | collective-permute-start | bytes 24584 | tf_op jit(solution)/shard_map/while/body/eval_jaxpr/ppermute | solution.py:16
  666.1 25.5 %collective-permute-start.2 = (f32[1,2048]{1,0:T(1,128)S(1)}, f32[1,2048]{1,0:T(1,128)S(1)}, u32[]{:S(2)}, u32[]{:S(2)}) collective-permute-start(f32[1,2048]{1,0:T(1,128)S(1)} %get-tuple-element.538), channel_id=1, source_target_pairs={{0,16},{16,32},{32,48},{48,64},{64,80},{80,96},{96,112},{112,0},{1... | collective-permute-start | bytes 24584 | tf_op jit(solution)/shard_map/while/body/eval_jaxpr/ppermute | solution.py:16
  691.9 11.6 %copy-start.1 = (bf16[2048,128]{1,0:T(8,128)(2,1)S(1)}, bf16[2048,128]{1,0:T(8,128)(2,1)}, u32[]{:S(2)}) copy-start(bf16[2048,128]{1,0:T(8,128)(2,1)} %get-tuple-element.578) | copy-start | bytes 1572868 | tf_op jit(solution)/shard_map/while
  710.4 32.1 %collective-permute-start.3 = (f32[1,2048,128]{2,1,0:T(8,128)}, f32[1,2048,128]{2,1,0:T(8,128)S(1)}, u32[]{:S(2)}, u32[]{:S(2)}) collective-permute-start(f32[1,2048,128]{2,1,0:T(8,128)} %fusion.71), channel_id=1, source_target_pairs={{0,16},{16,32},{32,48},{48,64},{64,80},{80,96},{96,112},{112,0},{1... | collective-permute-start | bytes 3145736 | tf_op jit(solution)/shard_map/while/body/eval_jaxpr/ppermute | solution.py:16
  710.4 32.1 %collective-permute-start = (bf16[1,2048,128]{2,1,0:T(8,128)(2,1)S(1)}, bf16[1,2048,128]{2,1,0:T(8,128)(2,1)S(1)}, u32[]{:S(2)}, u32[]{:S(2)}) collective-permute-start(bf16[1,2048,128]{2,1,0:T(8,128)(2,1)S(1)} %copy.25), channel_id=1, source_target_pairs={{0,16},{16,32},{32,48},{48,64},{64,80},{80,96},{96,112},{112,0},{1... | collective-permute-start | bytes 1572872 | tf_op jit(solution)/shard_map/while/body/eval_jaxpr/ppermute | solution.py:16
  713.3 29.1 %collective-permute-start.1 = (f32[1,2048]{1,0:T(1,128)S(1)}, f32[1,2048]{1,0:T(1,128)S(1)}, u32[]{:S(2)}, u32[]{:S(2)}) collective-permute-start(f32[1,2048]{1,0:T(1,128)S(1)} %max.14), channel_id=1, source_target_pairs={{0,16},{16,32},{32,48},{48,64},{64,80},{80,96},{96,112},{112,0},{1... | collective-permute-start | bytes 24584 | tf_op jit(solution)/shard_map/while/body/eval_jaxpr/ppermute | solution.py:16
  717.9 24.6 %collective-permute-start.2 = (f32[1,2048]{1,0:T(1,128)S(1)}, f32[1,2048]{1,0:T(1,128)S(1)}, u32[]{:S(2)}, u32[]{:S(2)}) collective-permute-start(f32[1,2048]{1,0:T(1,128)S(1)} %get-tuple-element.538), channel_id=1, source_target_pairs={{0,16},{16,32},{32,48},{48,64},{64,80},{80,96},{96,112},{112,0},{1... | collective-permute-start | bytes 24584 | tf_op jit(solution)/shard_map/while/body/eval_jaxpr/ppermute | solution.py:16
Sparse Core Ops, SparseCore 0:
  12.5 145.7 all-reduce.1
  162.7 147.8 reduce-scatter.1
where the time goes:
time: 756 us; the launch traced here: 750 us
  waiting for transfers between devices  491 us (65%)
  matrix products  108 us (14%)
  other arithmetic  70.4 us (9%)
  starting transfers between devices  56.3 us (7%)
  between operations  13.5 us (2%)
  local copies, waits for them, and re-layouts  10.7 us (1%)
    ppermute x32, waiting for transfers between devices, shifted(): lax.ppermute(array, axis, [(i, (i + by) % count) for i in range(count)])  221 us
    reduce_scatter x1, waiting for transfers between devices, on_device(): lax.psum_scatter(jnp.einsum('td,dhe->hte', hidden, columns, preferred_ele...  146 us
    psum x1, waiting for transfers between devices, on_device(): lax.psum(jnp.dot(hidden, w_key_value, preferred_element_type=jnp.float32)...  124 us
    reduce_sum x8, other arithmetic, attend_tile(): new_sum = run_sum * rescale + jnp.sum(weights_f, axis=-1)  59.6 us
    ppermute x32, starting transfers between devices, shifted(): lax.ppermute(array, axis, [(i, (i + by) % count) for i in range(count)])  56.3 us
    dot_general x8, matrix products, attend_tile(): jnp.einsum('hqk,ke->hqe', weights_f.astype(jnp.bfloat16), value_rows, pre...  55.3 us
    dot_general x8, matrix products, attend_tile(): jnp.einsum('hqe,ke->hqk', query_rows, key_rows, preferred_element_type=jn...  32.2 us
    dot_general x1, matrix products, on_device(): jnp.einsum('td,dhe->hte', hidden, columns, preferred_element_type=jnp.flo...  15.3 us
  transfers between devices with their start and end apart: 34, of which 18 were waited for; matrix products, arithmetic and copies ran while one was open for 4% of the time, Pallas kernels for 0%

commit v1 on v0

v1 whole, which is shorter than its diff:
```python
import jax
import jax.numpy as jnp
from jax import lax
from jax.sharding import PartitionSpec as P

DH = 128
HQ = 16
BLOCK = 512
MAX_DOC_BLOCKS = 16


masked_low = -1e30


def frequencies():
    half_dim = DH // 2
    return 500000.0 ** (-2.0 * jnp.arange(half_dim, dtype=jnp.float32) / DH)


def rotate_pairs(vectors, positions):
    half_dim = DH // 2
    angles = positions[:, None].astype(jnp.float32) * frequencies()[None, :]
    cosine = jnp.cos(angles)
    sine = jnp.sin(angles)
    first_half = vectors[..., :half_dim]
    second_half = vectors[..., half_dim:]
    return jnp.concatenate(
        [first_half * cosine - second_half * sine, second_half * cosine + first_half * sine], -1
    )


def document_of(positions, block_doc):
    block_ids = positions // BLOCK
    table_ids = jnp.arange(block_doc.shape[0], dtype=jnp.int32)
    matches = block_ids[:, None] == table_ids[None, :]
    return jnp.sum(jnp.where(matches, block_doc[None, :], 0), axis=1)


def attend_tile(state_in, query_rows, query_pos, query_doc, key_rows, value_rows, key_pos, key_doc, valid):
    allowed = (key_pos[None, :] <= query_pos[:, None]) & (query_doc[:, None] == key_doc[None, :]) & valid
    scale = DH ** (-0.5)
    run_max, run_sum, run_out = state_in
    scores = (
        jnp.einsum("hqe,ke->hqk", query_rows, key_rows, preferred_element_type=jnp.float32) * scale
    )
    scores = jnp.where(allowed[None], scores, masked_low)
    new_max = jnp.maximum(run_max, jnp.max(scores, axis=-1))
    weights_f = jnp.where(allowed[None], jnp.exp(scores - new_max[..., None]), 0.0)
    rescale = jnp.exp(run_max - new_max)
    new_sum = run_sum * rescale + jnp.sum(weights_f, axis=-1)
    new_out = run_out * rescale[..., None] + jnp.einsum(
        "hqk,ke->hqe",
        weights_f.astype(jnp.bfloat16),
        value_rows,
        preferred_element_type=jnp.float32,
    )
    return (new_max, new_sum, new_out)


def gather_fsdp(piece, n_fsdp):
    me = lax.axis_index("fsdp")
    bits = n_fsdp.bit_length() - 1
    held = piece
    for bit in reversed(range(bits)):
        pairs = [(i, i ^ (1 << bit)) for i in range(n_fsdp)]
        theirs = lax.ppermute(held, "fsdp", pairs)
        mine_first = ((me >> bit) & 1) == 0
        held = jnp.where(mine_first, jnp.stack([held, theirs]), jnp.stack([theirs, held]))
    held = jnp.transpose(held, tuple(reversed(range(bits))) + tuple(range(bits, held.ndim)))
    return held.reshape((n_fsdp,) + piece.shape)


def on_device(hidden, w_query, w_key_value, block_doc):
    tok_rows, feat_rows = hidden.shape
    n_fsdp = lax.axis_size("fsdp")
    n_ctx = lax.axis_size("ctx")
    quarter = DH // 2 // n_fsdp
    eighth = DH // n_fsdp
    w_keys = w_key_value[:, :DH]
    w_comb = jnp.concatenate(
        [
            w_query.reshape(feat_rows, n_fsdp, DH),
            w_keys[:, : DH // 2].reshape(feat_rows, n_fsdp, quarter),
            w_keys[:, DH // 2 :].reshape(feat_rows, n_fsdp, quarter),
            w_key_value[:, DH:].reshape(feat_rows, n_fsdp, eighth),
        ],
        axis=2,
    )
    reduced = lax.psum_scatter(
        jnp.einsum("td,dfc->ftc", hidden, w_comb, preferred_element_type=jnp.float32),
        "fsdp",
        scatter_dimension=0,
        tiled=True,
    )[0]
    me = lax.axis_index("ctx")
    me_f = lax.axis_index("fsdp")
    local_range = jnp.arange(tok_rows, dtype=jnp.int32)
    positions = me * tok_rows + local_range
    query = reduced[None, :, :DH]
    q_rot = rotate_pairs(query, positions).astype(jnp.bfloat16)
    key_a = reduced[:, DH : DH + quarter]
    key_b = reduced[:, DH + quarter : DH + 2 * quarter]
    vals = reduced[:, DH + 2 * quarter :]
    freq = lax.dynamic_slice_in_dim(frequencies(), me_f * quarter, quarter)
    angles = positions[:, None].astype(jnp.float32) * freq[None, :]
    cosine = jnp.cos(angles)
    sine = jnp.sin(angles)
    piece = jnp.concatenate(
        [key_a * cosine - key_b * sine, key_b * cosine + key_a * sine, vals], axis=1
    ).astype(jnp.bfloat16)
    gathered = gather_fsdp(piece, n_fsdp)
    gathered = jnp.transpose(gathered, (1, 0, 2))
    kv = jnp.concatenate(
        [
            gathered[:, :, :quarter].reshape(tok_rows, DH // 2),
            gathered[:, :, quarter : 2 * quarter].reshape(tok_rows, DH // 2),
            gathered[:, :, 2 * quarter :].reshape(tok_rows, DH),
        ],
        axis=1,
    )

    query_doc = document_of(positions, block_doc)
    reach = min((MAX_DOC_BLOCKS * BLOCK - 1 + tok_rows - 1) // tok_rows, n_ctx - 1)
    heads_dev = 1
    state = (
        jnp.full((heads_dev, tok_rows), masked_low, jnp.float32),
        jnp.zeros((heads_dev, tok_rows), jnp.float32),
        jnp.zeros((heads_dev, tok_rows, DH), jnp.float32),
    )
    for back in range(reach + 1):
        if back == 0:
            kv_here = kv
        else:
            kv_here = lax.ppermute(kv, "ctx", [(j, j + back) for j in range(n_ctx - back)])
        owner = me - back
        key_pos = owner * tok_rows + local_range
        key_doc = document_of(key_pos, block_doc)
        state = attend_tile(
            state, q_rot, positions, query_doc, kv_here[:, :DH], kv_here[:, DH:], key_pos, key_doc,
            owner >= 0,
        )
    run_max, run_sum, run_out = state
    attended = (run_out / run_sum[..., None]).astype(jnp.bfloat16)
    return jnp.transpose(attended, (1, 0, 2)).reshape(tok_rows, heads_dev * DH)


def solution(mesh):
    return jax.shard_map(
        on_device,
        mesh=mesh,
        in_specs=(P("ctx", "fsdp"), P("fsdp", None), P("fsdp", None), P()),
        out_specs=P("ctx", "fsdp"),
        check_vma=False,
    )
```

time: 756 us -> 474 us (0.63)
  waiting for transfers between devices: 491 us -> 252 us
  starting transfers between devices: 56.3 us -> 11.7 us
  other arithmetic: 70.4 us -> 34.3 us
  matrix products: 108 us -> 141 us
    ppermute x32 -> x8, waiting for transfers between devices: 221 us -> 95.7 us  [the longest x4 78.1 us: on_device(): lax.ppermute(kv, 'ctx', [(j, j + back) for j in range(n_ctx - back)])]
    psum x1 -> x0, waiting for transfers between devices: 124 us -> none  [on_device(): lax.psum(jnp.dot(hidden, w_key_value, preferred_element_type=jnp.float32)...]
    ppermute x32 -> x8, starting transfers between devices: 56.3 us -> 11.7 us  [the longest x4 8.46 us: on_device(): lax.ppermute(kv, 'ctx', [(j, j + back) for j in range(n_ctx - back)])]
    dot_general x8 -> x5, matrix products: 32.2 us -> 70.4 us  [attend_tile(): jnp.einsum('hqe,ke->hqk', query_rows, key_rows, preferred_element_type=jn...]
    reduce_sum x8 -> x1, other arithmetic: 59.6 us -> 29.7 us  [attend_tile(): new_sum = run_sum * rescale + jnp.sum(weights_f, axis=-1)]
    reduce_scatter x1, waiting for transfers between devices: 146 us -> 157 us  [on_device(): lax.psum_scatter(jnp.einsum('td,dfc->ftc', hidden, w_comb, preferred_elem...]
    dot_general x2 -> x1, matrix products: 20.1 us -> 16.7 us  [on_device(): jnp.einsum('td,dfc->ftc', hidden, w_comb, preferred_element_type=jnp.floa...]
    dot_general x8 -> x5, matrix products: 55.3 us -> 54 us  [attend_tile(): jnp.einsum('hqk,ke->hqe', weights_f.astype(jnp.bfloat16), value_rows, pre...]
  transfers between devices with their start and end apart: 34 -> 9, of which waited for: 18 -> 7; matrix products, arithmetic and copies ran while one was open for 4% -> 10% of each run, Pallas kernels for 0% -> 0%
where the time goes in v1:
time: 474 us; the launch traced here: 467 us
  waiting for transfers between devices  252 us (53%)
  matrix products  141 us (30%)
  other arithmetic  34.3 us (7%)
  between operations  14.3 us (3%)
  local copies, waits for them, and re-layouts  13.2 us (3%)
  starting transfers between devices  11.7 us (2%)
    reduce_scatter x1, waiting for transfers between devices, on_device(): lax.psum_scatter(jnp.einsum('td,dfc->ftc', hidden, w_comb, preferred_elem...  157 us
    ppermute x4, waiting for transfers between devices, on_device(): lax.ppermute(kv, 'ctx', [(j, j + back) for j in range(n_ctx - back)])  78.1 us
    dot_general x5, matrix products, attend_tile(): jnp.einsum('hqe,ke->hqk', query_rows, key_rows, preferred_element_type=jn...  70.4 us
    dot_general x5, matrix products, attend_tile(): jnp.einsum('hqk,ke->hqe', weights_f.astype(jnp.bfloat16), value_rows, pre...  54 us
    reduce_sum x1, other arithmetic, attend_tile(): new_sum = run_sum * rescale + jnp.sum(weights_f, axis=-1)  29.7 us
    ppermute x4, waiting for transfers between devices, gather_fsdp(): theirs = lax.ppermute(held, 'fsdp', pairs)  17.6 us
    dot_general x1, matrix products, on_device(): jnp.einsum('td,dfc->ftc', hidden, w_comb, preferred_element_type=jnp.floa...  16.7 us
  transfers between devices with their start and end apart: 9, of which 7 were waited for; matrix products, arithmetic and copies ran while one was open for 10% of the time, Pallas kernels for 0%

profile of v1, /device:TPU:40, one launch (start us, length us, event | category | flops | bytes accessed | tf_op | source)
XLA Modules:
  0.0 466.9 jit_solution(6433980604174535830)
XLA Ops:
  6.5 1.0 slice.67
  7.5 1.2 fusion.139
  8.7 0.1 copy.17
  8.9 0.1 copy.15
  9.0 0.1 reshape.929
  9.1 0.1 copy.16
  9.2 0.1 reshape.930
  9.3 6.4 %copy.14 = bf16[1024,2048]{0,1:T(8,128)(2,1)} copy(bf16[1024,2048]{1,0:T(8,128)(2,1)} %param.5) | data formatting | bytes 8388608 | tf_op args[1]
  15.7 16.7 %convolution_bitcast_fusion = f32[16,2048,144]{1,2,0:T(8,128)} fusion(bf16[1024,16,8]{0,2,1:T(8,128)(2,1)S(1)} %bitcast.68, bf16[1024,16,4]{0,2,1:T(4,128)(2,1)S(1)} %reshape.930, bf16[1024,16,4]{0,2,1:T(4,128)(2,1)S(1)} %reshape.929, bf16[1024,16,128]{0,2,1:T(8,128)(2,1)} %bitcast.51, bf16[2048,1024]{1,0:T(8,128)(2,1)} %param.4), kind=kOutput, calls=%fused_computation.35 | convolution fusion | flops 9682550784 | bytes 27787264 | tf_op jit(solution)/shard_map/td,dfc->ftc/dot_general | solution.py:90
  32.4 0.0 reduce-scatter.2.cloned.1.call-update
  32.5 0.1 dynamic_slice.3
  32.6 0.4 copy-done.2
  33.0 0.3 select_reduce_fusion
  33.3 156.5 %reduce-scatter.2.cloned.1.call-done = f32[1,2048,144]{1,2,0:T(8,128)} async-done(((f32[16,2048,144]{1,2,0:T(8,128)}), f32[1,2048,144]{1,2,0:T(8,128)}) %reduce-scatter.2.cloned.1.call-update) | async-done | bytes 1179664 | tf_op jit(solution)/shard_map/reduce_scatter | solution.py:89
  189.9 0.8 slice_bitcast_fusion.3
  190.7 0.8 slice.138
  191.6 1.2 fusion.98
  192.8 1.5 collective-permute-start
  194.4 4.3 collective-permute-done
  198.7 1.6 collective-permute-start.1
  200.3 5.2 %collective-permute-done.1 = bf16[2,2048,16]{1,2,0:T(8,128)(2,1)S(1)} collective-permute-done((bf16[2,2048,16]{1,2,0:T(8,128)(2,1)S(1)}, bf16[2,2048,16]{1,2,0:T(8,128)(2,1)S(1)}, u32[]{:S(2)}, u32[]{:S(2)}) %collective-permute-start.1) | collective-permute-done | bytes 131104 | tf_op jit(solution)/shard_map/ppermute | solution.py:66
  205.6 0.1 collective-permute-start.2
  205.7 6.3 %collective-permute-done.2 = bf16[2,2,2048,16]{2,3,1,0:T(8,128)(2,1)S(1)} collective-permute-done((bf16[2,2,2048,16]{2,3,1,0:T(8,128)(2,1)S(1)}, bf16[2,2,2048,16]{2,3,1,0:T(8,128)(2,1)S(1)}, u32[]{:S(2)}, u32[]{:S(2)}) %collective-permute-start.2) | collective-permute-done | bytes 262176 | tf_op jit(solution)/shard_map/ppermute | solution.py:66
  212.0 0.1 maximum_select_fusion.2
  212.1 0.1 collective-permute-start.3
  212.2 0.1 maximum_select_fusion.1
  212.3 1.8 collective-permute-done.3
  214.1 0.2 fusion.66
  214.3 0.1 copy.18
  214.4 0.3 fusion.138
  214.7 0.1 reshape.933
  214.8 0.1 reshape.934
  214.8 0.1 pad_maximum_fusion
  214.9 3.5 collective-permute-start.4
  218.4 1.3 slice_bitcast_fusion
  219.7 2.3 fusion.92
  222.0 1.3 collective-permute-start.7
  223.3 1.3 collective-permute-start.6
  224.6 2.4 collective-permute-start.5
  227.1 2.4 fusion.87
  229.4 13.5 %collective-permute-done.4 = bf16[2048,256]{0,1:T(8,128)(2,1)} collective-permute-done((bf16[2048,256]{0,1:T(8,128)(2,1)S(1)}, bf16[2048,256]{0,1:T(8,128)(2,1)}, u32[]{:S(2)}, u32[]{:S(2)}) %collective-permute-start.4) | collective-permute-done | bytes 1048608 | tf_op jit(solution)/shard_map/ppermute | solution.py:134
  243.0 3.4 fusion.85
  246.4 64.6 %collective-permute-done.5 = bf16[2048,256]{0,1:T(8,128)(2,1)} collective-permute-done((bf16[2048,256]{0,1:T(8,128)(2,1)S(1)}, bf16[2048,256]{0,1:T(8,128)(2,1)}, u32[]{:S(2)}, u32[]{:S(2)}) %collective-permute-start.5) | collective-permute-done | bytes 1048608 | tf_op jit(solution)/shard_map/ppermute | solution.py:134
  311.0 9.2 %fusion.82 = f32[2048,2048]{0,1:T(8,128)} fusion(bf16[2048,256]{0,1:T(8,128)(2,1)} %collective-permute-done.5, bf16[2048,64]{0,1:T(8,128)(2,1)S(1)} %get-tuple-element.32, bf16[2048,64]{0,1:T(8,128)(2,1)S(1)} %get-tuple-element.31), kind=kOutput, calls=%fused_computation.76 | convolution fusion | flops 1074790400 | bytes 17825792 | tf_op jit(solution)/shard_map/hqe,ke->hqk/dot_general | solution.py:44
  320.2 0.0 collective-permute-done.7
  320.2 28.2 %fusion.4 = (f32[2048]{0:T(1024)S(1)}, f32[2048]{0:T(1024)S(1)}, f32[2048]{0:T(1024)S(1)}, f32[2048]{0:T(1024)S(1)}, f32[2048,2048]{0,1:T(8,128)}) fusion(pred[]{:T(512)S(6)} %ge.19, s32[2048]{0:T(1024)S(1)} %get-tuple-element.15, s32[2048]{0:T(1024)S(1)} %get-tuple-element.19, s32[2048]{0:T(1024)S(1)} %get-tuple-element.48, ...), kind=kOutput, calls=%fused_computation.19 | convolution fusion | flops 1192222720 | bytes 68272128 | tf_op jit(solution)/shard_map/hqe,ke->hqk/dot_general | solution.py:44
  348.4 0.0 collective-permute-done.6
  348.4 0.0 copy-done.1
  348.4 27.3 %fusion.7 = (f32[2048]{0:T(1024)S(1)}, f32[2048]{0:T(1024)S(1)}, f32[2048]{0:T(1024)S(1)}, f32[2048,2048]{0,1:T(8,128)}) fusion(f32[2048,2048]{0,1:T(8,128)S(1)} %fusion.85, f32[2048]{0:T(1024)S(1)} %get-tuple-element.28, pred[]{:T(512)S(6)} %ge.16, s32[2048]{0:T(1024)S(1)} %get-tuple-element.16, s32[2048]{0:T(1024)S(1)} %get-tuple-element.19, ...), kind=kOutput, calls=%fused_computation.22 | convolution fusion | flops 1179641856 | bytes 51486724 | tf_op jit(solution)/shard_map/hqe,ke->hqk/dot_general | solution.py:44
  375.7 0.0 slice-start.5
  375.7 29.7 %fusion.5 = (f32[2048]{0:T(1024)S(1)}, f32[2048]{0:T(1024)S(1)}, f32[2048]{0:T(1024)S(1)}) fusion(f32[2048,2048]{0,1:T(8,128)} %copy-done, f32[2048]{0:T(1024)S(1)} %get-tuple-element.38, pred[]{:T(512)S(6)} %ge.15, s32[2048]{0:T(1024)S(1)} %get-tuple-element.19, s32[2048]{0:T(1024)S(1)} %get-tuple-element.48, f32[2048]{0:T(1024)S(1)} %get-tuple-element.25, ...), kind=kLoop, calls=%fused_computation.20 | loop fusion | flops 113240064 | bytes 50429956 | tf_op jit(solution)/shard_map/reduce_sum | solution.py:50
  405.4 0.0 slice-start.6
  405.4 0.0 slice-start.7
  405.5 12.3 %fusion.36 = f32[2048,128]{1,0:T(8,128)S(1)} fusion(f32[2048,2048]{0,1:T(8,128)} %copy-done, f32[2048]{0:T(1024)S(1)} %get-tuple-element.38, pred[]{:T(512)S(6)} %ge.15, s32[2048]{0:T(1024)S(1)} %get-tuple-element.19, s32[2048]{0:T(1024)S(1)} %get-tuple-element.48, f32[2048]{0:T(1024)S(1)} %get-tuple-element.24, f32[2048]{0:T(1024)S(1)} %get-tuple-element.37, ...), kind=kOutput, calls=%fused_computation.45 | convolution fusion | flops 1112014848 | bytes 18407424 | tf_op jit(solution)/shard_map/hqk,ke->hqe/dot_general | solution.py:51
  417.8 8.5 %fusion.19 = f32[2048,128]{1,0:T(8,128)S(1)} fusion(f32[2048,2048]{0,1:T(8,128)S(1)} %bitcast.50, f32[2048]{0:T(1024)S(1)} %get-tuple-element.27, bf16[2048,256]{0,1:T(8,128)(2,1)} %collective-permute-done.5, s32[2048]{0:T(1024)S(1)} %get-tuple-element.19, s32[2048]{0:T(1024)S(1)} %get-tuple-element.48, s32[2048]{0:T(1024)S(1)} %get-tuple-element.17, ...), kind=kOutput, calls=%fused_computation.32 | convolution fusion | flops 1111490560 | bytes 18391040 | tf_op jit(solution)/shard_map/hqk,ke->hqe/dot_general | solution.py:51
  426.3 0.0 slice-start
  426.4 0.0 slice-start.1
  426.4 11.3 %fusion.15 = f32[2048,128]{1,0:T(8,128)S(1)} fusion(f32[2048,2048]{0,1:T(8,128)} %get-tuple-element.39, f32[2048]{0:T(1024)S(1)} %get-tuple-element.25, bf16[2048,256]{0,1:T(8,128)(2,1)} %collective-permute-done.7, s32[2048]{0:T(1024)S(1)} %get-tuple-element.19, s32[2048]{0:T(1024)S(1)} %get-tuple-element.48, s32[2048]{0:T(1024)S(1)} %get-tuple-element.15, ...), kind=kOutput, calls=%fused_computation.30 | convolution fusion | flops 1111490560 | bytes 18391040 | tf_op jit(solution)/shard_map/hqk,ke->hqe/dot_general | solution.py:51
  437.7 0.0 slice-start.2
  437.7 0.0 slice-start.3
  437.7 11.5 %fusion.17 = f32[2048,128]{1,0:T(8,128)S(1)} fusion(f32[2048,2048]{0,1:T(8,128)} %get-tuple-element.40, f32[2048]{0:T(1024)S(1)} %get-tuple-element.26, bf16[2048,256]{0,1:T(8,128)(2,1)} %collective-permute-done.6, s32[2048]{0:T(1024)S(1)} %get-tuple-element.19, s32[2048]{0:T(1024)S(1)} %get-tuple-element.48, s32[2048]{0:T(1024)S(1)} %get-tuple-element.18, ...), kind=kOutput, calls=%fused_computation.31 | convolution fusion | flops 1111490560 | bytes 18391040 | tf_op jit(solution)/shard_map/hqk,ke->hqe/dot_general | solution.py:51
  449.2 0.0 slice-done
  449.2 0.0 slice-done.1
  449.3 10.3 %fusion.63 = bf16[2048,128]{1,0:T(8,128)(2,1)} fusion(f32[2048,128]{1,0:T(8,128)S(1)} %fusion.15, f32[2048,128]{1,0:T(8,128)S(1)} %fusion.17, f32[2048,128]{1,0:T(8,128)S(1)} %fusion.19, f32[2048,128]{1,0:T(8,128)S(1)} %fusion.36, f32[2048,2048]{0,1:T(8,128)S(1)} %bitcast.48, f32[2048]{0:T(1024)S(1)} %get-tuple-element.28, ...), kind=kOutput, calls=%fused_computation.54 | convolution fusion | flops 1113849856 | bytes 22093824 | tf_op jit(solution)/shard_map/hqk,ke->hqe/dot_general | solution.py:51
  (34 shorter events, 0.4 us)
Async XLA Ops:
  6.5 183.3 %reduce-scatter.2.cloned.1.call-start = ((), (), s32[]{:S(2)}) async-start(), calls=%async_computation.1 | async-start | bytes 20054016 | tf_op jit(solution)/shard_map/reduce_scatter | solution.py:89
  32.4 0.7 copy-start.2
  192.8 5.8 %collective-permute-start = (bf16[2048,16]{0,1:T(8,128)(2,1)S(1)}, bf16[2048,16]{0,1:T(8,128)(2,1)S(1)}, u32[]{:S(2)}, u32[]{:S(2)}) collective-permute-start(bf16[2048,16]{0,1:T(8,128)(2,1)S(1)} %pad_maximum_fusion.2), channel_id=1, source_target_pairs={{0,8},{1,9},{2,10},{3,11},{4,12},{5,13},{6,14},{7,15},{8,0},{9,1},... | collective-permute-start | bytes 196616 | tf_op jit(solution)/shard_map/ppermute | solution.py:66
  198.7 6.8 %collective-permute-start.1 = (bf16[2,2048,16]{1,2,0:T(8,128)(2,1)S(1)}, bf16[2,2048,16]{1,2,0:T(8,128)(2,1)S(1)}, u32[]{:S(2)}, u32[]{:S(2)}) collective-permute-start(bf16[2,2048,16]{1,2,0:T(8,128)(2,1)S(1)} %maximum_select_fusion.6), channel_id=1, source_target_pairs={{0,4},{1,5},{2,6},{3,7},{4,0},{5,1},{6,2},{7,3},{8,12},{9,13},{10,... | collective-permute-start | bytes 393224 | tf_op jit(solution)/shard_map/ppermute | solution.py:66
  205.6 6.5 %collective-permute-start.2 = (bf16[2,2,2048,16]{2,3,1,0:T(8,128)(2,1)S(1)}, bf16[2,2,2048,16]{2,3,1,0:T(8,128)(2,1)S(1)}, u32[]{:S(2)}, u32[]{:S(2)}) collective-permute-start(bf16[2,2,2048,16]{2,3,1,0:T(8,128)(2,1)S(1)} %maximum_select_fusion.4), channel_id=1, source_target_pairs={{0,2},{1,3},{2,0},{3,1},{4,6},{5,7},{6,4},{7,5},{8,10},{9,11},{10,... | collective-permute-start | bytes 786440 | tf_op jit(solution)/shard_map/ppermute | solution.py:66
  212.1 2.0 collective-permute-start.3
  214.9 28.0 %collective-permute-start.4 = (bf16[2048,256]{0,1:T(8,128)(2,1)S(1)}, bf16[2048,256]{0,1:T(8,128)(2,1)}, u32[]{:S(2)}, u32[]{:S(2)}) collective-permute-start(bf16[2048,256]{0,1:T(8,128)(2,1)S(1)} %pad_maximum_fusion), channel_id=1, source_target_pairs={{0,16},{16,32},{32,48},{48,64},{64,80},{80,96},{96,112},{1,17},{17... | collective-permute-start | bytes 3145736 | tf_op jit(solution)/shard_map/ppermute | solution.py:134
  222.0 98.1 %collective-permute-start.7 = (bf16[2048,256]{0,1:T(8,128)(2,1)S(1)}, bf16[2048,256]{0,1:T(8,128)(2,1)}, u32[]{:S(2)}, u32[]{:S(2)}) collective-permute-start(bf16[2048,256]{0,1:T(8,128)(2,1)S(1)} %pad_maximum_fusion), channel_id=1, source_target_pairs={{0,64},{16,80},{32,96},{48,112},{1,65},{17,81},{33,97},{49,113},{2... | collective-permute-start | bytes 3145736 | tf_op jit(solution)/shard_map/ppermute | solution.py:134
  223.3 125.0 %collective-permute-start.6 = (bf16[2048,256]{0,1:T(8,128)(2,1)S(1)}, bf16[2048,256]{0,1:T(8,128)(2,1)}, u32[]{:S(2)}, u32[]{:S(2)}) collective-permute-start(bf16[2048,256]{0,1:T(8,128)(2,1)S(1)} %pad_maximum_fusion), channel_id=1, source_target_pairs={{0,48},{16,64},{32,80},{48,96},{64,112},{1,49},{17,65},{33,81},{49... | collective-permute-start | bytes 3145736 | tf_op jit(solution)/shard_map/ppermute | solution.py:134
  224.6 86.3 %collective-permute-start.5 = (bf16[2048,256]{0,1:T(8,128)(2,1)S(1)}, bf16[2048,256]{0,1:T(8,128)(2,1)}, u32[]{:S(2)}, u32[]{:S(2)}) collective-permute-start(bf16[2048,256]{0,1:T(8,128)(2,1)S(1)} %pad_maximum_fusion), channel_id=1, source_target_pairs={{0,32},{16,48},{32,64},{48,80},{64,96},{80,112},{1,33},{17,49},{33... | collective-permute-start | bytes 3145736 | tf_op jit(solution)/shard_map/ppermute | solution.py:134
  229.4 90.7 %copy-start = (f32[2048,2048]{0,1:T(8,128)}, f32[2048,2048]{0,1:T(8,128)S(1)}, u32[]{:S(2)}) copy-start(f32[2048,2048]{0,1:T(8,128)S(1)} %fusion.87) | copy-start | bytes 50331652
  246.4 102.0 %copy-start.1 = (f32[2048,2048]{0,1:T(8,128)}, f32[2048,2048]{0,1:T(8,128)S(1)}, u32[]{:S(2)}) copy-start(f32[2048,2048]{0,1:T(8,128)S(1)} %fusion.85) | copy-start | bytes 50331652
  375.6 42.1 %slice-start.4 = ((s8[16777216]{0:T(1024)(128)(4,1)}), s8[4194304]{0:T(1024)(128)(4,1)S(1)}, s32[]{:S(2)}) async-start(s8[16777216]{0:T(1024)(128)(4,1)} %bitcast.49), calls=%async_computation.6 | async-start | bytes 8388608
  375.7 42.1 %slice-start.5 = ((s8[16777216]{0:T(1024)(128)(4,1)}), s8[4194304]{0:T(1024)(128)(4,1)S(1)}, s32[]{:S(2)}) async-start(s8[16777216]{0:T(1024)(128)(4,1)} %bitcast.49), calls=%async_computation.7 | async-start | bytes 8388608
  405.4 12.4 %slice-start.6 = ((s8[16777216]{0:T(1024)(128)(4,1)}), s8[4194304]{0:T(1024)(128)(4,1)S(1)}, s32[]{:S(2)}) async-start(s8[16777216]{0:T(1024)(128)(4,1)} %bitcast.49), calls=%async_computation.8 | async-start | bytes 8388608
  405.4 12.4 %slice-start.7 = ((s8[16777216]{0:T(1024)(128)(4,1)}), s8[4194304]{0:T(1024)(128)(4,1)S(1)}, s32[]{:S(2)}) async-start(s8[16777216]{0:T(1024)(128)(4,1)} %bitcast.49), calls=%async_computation.9 | async-start | bytes 8388608
  426.3 22.9 %slice-start = ((s8[16777216]{0:T(1024)(128)(4,1)}), s8[4194304]{0:T(1024)(128)(4,1)S(1)}, s32[]{:S(2)}) async-start(s8[16777216]{0:T(1024)(128)(4,1)} %bitcast.47), calls=%async_computation.2 | async-start | bytes 8388608
  426.4 22.9 %slice-start.1 = ((s8[16777216]{0:T(1024)(128)(4,1)}), s8[4194304]{0:T(1024)(128)(4,1)S(1)}, s32[]{:S(2)}) async-start(s8[16777216]{0:T(1024)(128)(4,1)} %bitcast.47), calls=%async_computation.3 | async-start | bytes 8388608
  437.7 11.6 %slice-start.2 = ((s8[16777216]{0:T(1024)(128)(4,1)}), s8[4194304]{0:T(1024)(128)(4,1)S(1)}, s32[]{:S(2)}) async-start(s8[16777216]{0:T(1024)(128)(4,1)} %bitcast.47), calls=%async_computation.4 | async-start | bytes 8388608
  437.7 11.6 %slice-start.3 = ((s8[16777216]{0:T(1024)(128)(4,1)}), s8[4194304]{0:T(1024)(128)(4,1)S(1)}, s32[]{:S(2)}) async-start(s8[16777216]{0:T(1024)(128)(4,1)} %bitcast.47), calls=%async_computation.5 | async-start | bytes 8388608
Sparse Core Ops, SparseCore 0:
  32.5 157.2 reduce-scatter.1
